TPU v7x, 512 devices: a whole 4x4x16 slice. The times are simulated.
512 devices in a mesh: segment: 8 (over y_hi, x), dp: 64 (over y_lo, z, core).
Axes of the slice: x: 4, y: 4 (y_hi: 2, y_lo: 2; y = y_hi * 2 + y_lo), z: 16, core: 2. Of those that a mesh axis runs over, the one named last changes fastest.
Arguments:
- acts: bfloat16 [8, 128, 4, 8, 8, 128], P('segment', 'dp'), may hold values from -6 to 6
- weights: bfloat16 [8, 3456, 128], P('segment', 'dp'), may hold values from -0.109375 to 0.109375
- pos_weight: float32 [8, 3, 128], P('segment'), may hold values from -4 to 4
- anchors: int32 [128, 3], P('dp'), may hold values from 0 to 1983
- top_grad: bfloat16 [128, 4, 8, 8, 128], P('dp'), may hold values from -6 to 6
Outputs:
- section_grads: bfloat16 [8, 128, 4, 8, 8, 128], P('segment', 'dp')
- weight_grad: float32 [8, 3456, 128], P('segment', 'dp')
Inputs may be any that keep to these rules, and one draw needn't show every extreme that they name: `anchors`: mesh coordinates of each crop's corner.
All inputs are finite; a program needn't handle non-finite values.
Results may differ from a plain program's by a relative error of at most 0.015.
Values may be sent and summed in bfloat16 or wider, within the bound.
No kernel may reach another device: no remote copies, remote signals or barrier semaphores. Data moves between devices by JAX's collectives and lax.ppermute only.
A program may use at most 64 MiB of HBM per device.

v0:
```python
import math
import jax
import jax.numpy as jnp
from jax import lax
from jax.sharding import PartitionSpec as P

STRIDE = 2
WAVE = 64


def passed_along(array, axis, by):
    length = lax.axis_size(axis)
    pairs = [(i, i + by) for i in range(length) if 0 <= i + by < length]
    return lax.ppermute(array, axis, pairs)


def apply_taps(field, kernel_taps):
    size_x, size_y, size_z, channels = field.shape
    padded = jnp.pad(field, ((1, 1), (1, 1), (1, 1), (0, 0)))
    summed = jnp.zeros((size_x * size_y * size_z, kernel_taps.shape[2]), jnp.float32)
    tap_index = 0
    for first in range(3):
        for second in range(3):
            for third in range(3):
                window_rows = padded[
                    first : first + size_x, second : second + size_y, third : third + size_z
                ].reshape(size_x * size_y * size_z, channels)
                summed = summed + jnp.dot(
                    window_rows, kernel_taps[tap_index], preferred_element_type=jnp.float32
                )
                tap_index += 1
    return summed


def tap_grads(field, slope):
    size_x, size_y, size_z, channels = field.shape
    padded = jnp.pad(field, ((1, 1), (1, 1), (1, 1), (0, 0)))
    blocks = []
    for first in range(3):
        for second in range(3):
            for third in range(3):
                window_rows = padded[
                    first : first + size_x, second : second + size_y, third : third + size_z
                ].reshape(size_x * size_y * size_z, channels)
                blocks.append(jnp.dot(window_rows.T, slope, preferred_element_type=jnp.float32))
    return jnp.concatenate(blocks, axis=0)


def position_term(anchor, pos_gain, size_x, size_y, size_z):
    phases = []
    for axis_num, axis_len in enumerate((size_x, size_y, size_z)):
        coords = anchor[axis_num] + STRIDE * jnp.arange(axis_len, dtype=jnp.int32)
        phase_val = (coords % WAVE).astype(jnp.float32)
        phases.append(jnp.sin(phase_val * (2.0 * math.pi / WAVE)))
    position_sum = (
        phases[0][:, None, None, None] * pos_gain[0]
        + phases[1][None, :, None, None] * pos_gain[1]
        + phases[2][None, None, :, None] * pos_gain[2]
    )
    return position_sum.reshape(size_x * size_y * size_z, pos_gain.shape[1])


def layer_slope(incoming_rows, pre_act):
    sigmoid_h = jax.nn.sigmoid(pre_act)
    silu_slope = sigmoid_h * (1.0 + pre_act * (1.0 - sigmoid_h))
    return (incoming_rows * silu_slope).astype(jnp.bfloat16)


def local(acts, weights, pos_weight, anchors, top_grad):
    segments = lax.axis_size("segment")
    dp_count = lax.axis_size("dp")
    segment_index = lax.axis_index("segment")
    gathered = lax.all_gather(weights[0], "dp", axis=0, tiled=True)
    channels = gathered.shape[1]
    kernel_taps = gathered.reshape(-1, channels, channels)
    flipped = jnp.transpose(jnp.flip(kernel_taps, 0), (0, 2, 1))
    inputs_local = acts[0]
    micro_count = inputs_local.shape[0]
    size_x, size_y, size_z = (inputs_local.shape[1], inputs_local.shape[2], inputs_local.shape[3])
    cell_count = size_x * size_y * size_z
    rows_local = weights.shape[1]
    pos_gain = pos_weight[0]
    position_all = jnp.stack(
        [
            position_term(anchors[micro], pos_gain, size_x, size_y, size_z)
            for micro in range(micro_count)
        ]
    )
    tick_count = segments + micro_count - 1
    scale_factor = 1.0 / math.sqrt(dp_count * micro_count * cell_count)

    def tick_step(step_num, carry):
        incoming, grads_held, slopes_held, accumulated = carry
        micro_index = step_num - (segments - 1 - segment_index)
        active = (micro_index >= 0) & (micro_index < micro_count)
        slot_index = jnp.clip(micro_index, 0, micro_count - 1)

        def busy_work(operands):
            incoming_in, grads_in, slopes_in = operands
            top_slice = lax.dynamic_index_in_dim(top_grad, slot_index, 0, keepdims=False)
            cotangent = jnp.where(segment_index == segments - 1, top_slice, incoming_in)
            field = lax.dynamic_index_in_dim(inputs_local, slot_index, 0, keepdims=False)
            pre_act = apply_taps(field, kernel_taps) + lax.dynamic_index_in_dim(
                position_all, slot_index, 0, keepdims=False
            )
            incoming_rows = cotangent.reshape(cell_count, channels).astype(jnp.float32)
            slope = layer_slope(incoming_rows, pre_act)
            down_grad = (
                incoming_rows + apply_taps(slope.reshape(size_x, size_y, size_z, channels), flipped)
            ).astype(jnp.bfloat16)
            down_grad = down_grad.reshape(size_x, size_y, size_z, channels)
            grads_out = lax.dynamic_update_index_in_dim(grads_in, down_grad, slot_index, 0)
            slopes_out = lax.dynamic_update_index_in_dim(slopes_in, slope, slot_index, 0)
            grad_term = jnp.zeros((1, channels), jnp.float32)
            return (down_grad, grads_out, slopes_out, grad_term)

        def quiet_work(operands):
            incoming_in, grads_in, slopes_in = operands
            grad_term = jnp.zeros((1, channels), jnp.float32)
            return (jnp.zeros_like(incoming_in), grads_in, slopes_in, grad_term)

        down_grad, grads_held, slopes_held, grad_term = lax.cond(
            active, busy_work, quiet_work, (incoming, grads_held, slopes_held)
        )
        incoming = passed_along(down_grad, "segment", -1)
        return (incoming, grads_held, slopes_held, accumulated)

    start_carry = (
        jnp.zeros((size_x, size_y, size_z, channels), jnp.bfloat16),
        jnp.zeros(inputs_local.shape, jnp.bfloat16),
        jnp.zeros((micro_count, cell_count, channels), jnp.bfloat16),
        jnp.zeros((rows_local, channels), jnp.float32),
    )
    incoming, grads_held, slopes_held, accumulated = lax.fori_loop(
        0, tick_count, tick_step, start_carry
    )
    grad_term = tap_grads(inputs_local[0], slopes_held[0])
    micro = 1
    grad_term = grad_term + tap_grads(inputs_local[micro], slopes_held[micro])
    reduced = lax.psum_scatter(grad_term, "dp", scatter_dimension=0, tiled=True)
    return (grads_held[None], (reduced * scale_factor)[None])


def solution(mesh):
    return jax.shard_map(
        local,
        mesh=mesh,
        in_specs=(
            P("segment", "dp", None, None, None, None),
            P("segment", "dp", None),
            P("segment", None, None),
            P("dp", None),
            P("dp", None, None, None, None),
        ),
        out_specs=(P("segment", "dp", None, None, None, None), P("segment", "dp", None)),
        check_vma=False,
    )
```

profile of v0, /device:TPU:1, one launch (start us, length us, event | category | flops | bytes accessed | tf_op | source)
XLA Modules:
  0.0 428.4 jit_solution(7778404728182434695)
XLA Ops:
  0.6 1.6 fusion.250
  5.3 75.9 %all-gather = bf16[1,3456,128]{2,0,1:T(2,128)(2,1)S(1)} all-gather(bf16[1,54,128]{2,0,1:T(2,128)(2,1)S(1)} %copy.12), channel_id=2, replica_groups=mesh['segment'=8,'dp'=64] {'dp'}, dimensions={1}, use_global_device_ids=true | all-gather | bytes 898560 | tf_op jit(solution)/shard_map/all_gather | solution.py:73
  89.9 157.1 %while.18 = (s32[]{:T(128)}, bf16[4,8,8,128]{3,2,1,0:T(8,128)(2,1)S(1)}, bf16[2,4,8,8,128]{4,3,2,1,0:T(8,128)(2,1)}, bf16[2,256,128]{2,1,0:T(8,128)(2,1)S(1)}, s...) while((s32[]{:T(128)}, ...), condition=%wide.region_3.4_spmd, body=%wide.region_0.3_spmd.sunk | while | flops 455180288 | bytes 23921024 | solution.py:134
  91.9 4.3 %collective-permute-done = bf16[4,8,8,128]{3,2,1,0:T(8,128)(2,1)S(1)} collective-permute-done((bf16[4,8,8,128]{3,2,1,0:T(8,128)(2,1)}, bf16[4,8,8,128]{3,2,1,0:T(8,128)(2,1)S(1)}, u32[]{:S(2)}, u32[]{:S(2)}) %collective-permute-start) | collective-permute-done | bytes 65568 | tf_op jit(solution)/shard_map/while/body/eval_jaxpr/ppermute | solution.py:14
  98.2 3.9 collective-permute-done
  104.1 3.9 collective-permute-done
  109.9 6.5 %collective-permute-done = bf16[4,8,8,128]{3,2,1,0:T(8,128)(2,1)S(1)} collective-permute-done((bf16[4,8,8,128]{3,2,1,0:T(8,128)(2,1)}, bf16[4,8,8,128]{3,2,1,0:T(8,128)(2,1)S(1)}, u32[]{:S(2)}, u32[]{:S(2)}) %collective-permute-start) | collective-permute-done | bytes 65568 | tf_op jit(solution)/shard_map/while/body/eval_jaxpr/ppermute | solution.py:14
  118.4 7.5 %collective-permute-done = bf16[4,8,8,128]{3,2,1,0:T(8,128)(2,1)S(1)} collective-permute-done((bf16[4,8,8,128]{3,2,1,0:T(8,128)(2,1)}, bf16[4,8,8,128]{3,2,1,0:T(8,128)(2,1)S(1)}, u32[]{:S(2)}, u32[]{:S(2)}) %collective-permute-start) | collective-permute-done | bytes 65568 | tf_op jit(solution)/shard_map/while/body/eval_jaxpr/ppermute | solution.py:14
  127.8 7.5 %collective-permute-done = bf16[4,8,8,128]{3,2,1,0:T(8,128)(2,1)S(1)} collective-permute-done((bf16[4,8,8,128]{3,2,1,0:T(8,128)(2,1)}, bf16[4,8,8,128]{3,2,1,0:T(8,128)(2,1)S(1)}, u32[]{:S(2)}, u32[]{:S(2)}) %collective-permute-start) | collective-permute-done | bytes 65568 | tf_op jit(solution)/shard_map/while/body/eval_jaxpr/ppermute | solution.py:14
  137.3 71.9 %collective-permute-done = bf16[4,8,8,128]{3,2,1,0:T(8,128)(2,1)S(1)} collective-permute-done((bf16[4,8,8,128]{3,2,1,0:T(8,128)(2,1)}, bf16[4,8,8,128]{3,2,1,0:T(8,128)(2,1)S(1)}, u32[]{:S(2)}, u32[]{:S(2)}) %collective-permute-start) | collective-permute-done | bytes 65568 | tf_op jit(solution)/shard_map/while/body/eval_jaxpr/ppermute | solution.py:14
  209.2 11.9 %conditional.2 = (bf16[4,8,8,128]{3,2,1,0:T(8,128)(2,1)}, bf16[2,4,8,8,128]{4,3,2,1,0:T(8,128)(2,1)}, bf16[2,256,128]{2,1,0:T(8,128)(2,1)S(1)}) conditional(s32[]{:T(128)} %convert_element_type.107, (bf16[2,4,8,8,128]{4,3,2,1,0:T(8,128)(2,1)}, bf16[2,256,128]{2,1,0:T(8,128)(2,1)S(1)}) %tuple.170, (s32[]{:T(128)}, s32[]{:T(128)}, ...), branch_computations={%region_1.1_spmd, %region_2.2_spmd} | conditional | flops 455180288 | bytes 23658574 | solution.py:122
  219.6 1.5 constant_dynamic-update-slice_fusion
  222.4 7.5 %collective-permute-done = bf16[4,8,8,128]{3,2,1,0:T(8,128)(2,1)S(1)} collective-permute-done((bf16[4,8,8,128]{3,2,1,0:T(8,128)(2,1)}, bf16[4,8,8,128]{3,2,1,0:T(8,128)(2,1)S(1)}, u32[]{:S(2)}, u32[]{:S(2)}) %collective-permute-start) | collective-permute-done | bytes 65568 | tf_op jit(solution)/shard_map/while/body/eval_jaxpr/ppermute | solution.py:14
  229.9 11.9 %conditional.2 = (bf16[4,8,8,128]{3,2,1,0:T(8,128)(2,1)}, bf16[2,4,8,8,128]{4,3,2,1,0:T(8,128)(2,1)}, bf16[2,256,128]{2,1,0:T(8,128)(2,1)S(1)}) conditional(s32[]{:T(128)} %convert_element_type.107, (bf16[2,4,8,8,128]{4,3,2,1,0:T(8,128)(2,1)}, bf16[2,256,128]{2,1,0:T(8,128)(2,1)S(1)}) %tuple.170, (s32[]{:T(128)}, s32[]{:T(128)}, ...), branch_computations={%region_1.1_spmd, %region_2.2_spmd} | conditional | flops 455180288 | bytes 23658574 | solution.py:122
  243.2 3.9 collective-permute-done
  258.7 122.4 %fusion = f32[64,128]{1,0:T(8,128)S(1)} fusion(f32[3456,128]{1,0:T(8,128)S(1)} %add.436), kind=kCustom, calls=%all-reduce-scatter | all-reduce-scatter fusion | flops 524289 | bytes 1804288
  385.0 11.3 %collective-permute-start.6 = (f32[64,128]{1,0:T(8,128)S(1)}, f32[64,128]{1,0:T(8,128)S(1)}, u32[]{:S(2)}, u32[]{:S(2)}) collective-permute-start(f32[64,128]{1,0:T(8,128)S(1)} %fusion), channel_id=1, source_target_pairs={{0,6},{1,7},{2,8},{3,9},{4,10},{5,11},{6,12},{7,13},{8,14},{9,15},... | collective-permute-start | bytes 98312
  396.3 6.0 %collective-permute-start.10 = (f32[54,128]{1,0:T(8,128)S(1)}, f32[54,128]{1,0:T(8,128)S(1)}, u32[]{:S(2)}, u32[]{:S(2)}) collective-permute-start(f32[54,128]{1,0:T(8,128)S(1)} %slice.604), channel_id=1, source_target_pairs={{0,10},{1,11},{2,12},{3,13},{4,14},{5,15},{6,16},{7,17},{8,18},{9,... | collective-permute-start | bytes 82952
  402.2 1.7 collective-permute-done.10
  404.0 2.0 collective-permute-start.5
  406.0 9.6 %collective-permute-start.4 = (f32[64,128]{1,0:T(8,128)S(1)}, f32[64,128]{1,0:T(8,128)S(1)}, u32[]{:S(2)}, u32[]{:S(2)}) collective-permute-start(f32[64,128]{1,0:T(8,128)S(1)} %fusion), channel_id=1, source_target_pairs={{0,4},{1,5},{2,6},{3,7},{4,8},{5,9},{6,10},{7,11},{8,12},{9,13},{1... | collective-permute-start | bytes 98312
  416.9 3.1 collective-permute-start.2
  420.1 4.0 collective-permute-start.1
  426.1 1.7 concatenate.8
  (346 shorter events, 72.0 us)
Async XLA Ops:
  89.9 158.1 %copy-start.42 = (bf16[4,8,8,128]{3,2,1,0:T(8,128)(2,1)S(1)}, bf16[4,8,8,128]{3,2,1,0:T(8,128)(2,1)}, u32[]{:S(2)}) copy-start(bf16[4,8,8,128]{3,2,1,0:T(8,128)(2,1)} %get-tuple-element.394) | copy-start | bytes 196612
  89.9 158.3 %copy-start.41 = (bf16[4,8,8,128]{3,2,1,0:T(8,128)(2,1)S(1)}, bf16[4,8,8,128]{3,2,1,0:T(8,128)(2,1)}, u32[]{:S(2)}) copy-start(bf16[4,8,8,128]{3,2,1,0:T(8,128)(2,1)} %get-tuple-element.395) | copy-start | bytes 196612
  89.9 158.5 %copy-start.40 = (bf16[4,8,8,128]{3,2,1,0:T(8,128)(2,1)S(1)}, bf16[4,8,8,128]{3,2,1,0:T(8,128)(2,1)}, u32[]{:S(2)}) copy-start(bf16[4,8,8,128]{3,2,1,0:T(8,128)(2,1)} %get-tuple-element.396) | copy-start | bytes 196612
  89.9 158.7 %copy-start.39 = (bf16[4,8,8,128]{3,2,1,0:T(8,128)(2,1)S(1)}, bf16[4,8,8,128]{3,2,1,0:T(8,128)(2,1)}, u32[]{:S(2)}) copy-start(bf16[4,8,8,128]{3,2,1,0:T(8,128)(2,1)} %get-tuple-element.397) | copy-start | bytes 196612
  89.9 158.9 %copy-start.38 = (bf16[4,8,8,128]{3,2,1,0:T(8,128)(2,1)S(1)}, bf16[4,8,8,128]{3,2,1,0:T(8,128)(2,1)}, u32[]{:S(2)}) copy-start(bf16[4,8,8,128]{3,2,1,0:T(8,128)(2,1)} %get-tuple-element.398) | copy-start | bytes 196612
  90.6 5.6 %collective-permute-start = (bf16[4,8,8,128]{3,2,1,0:T(8,128)(2,1)}, bf16[4,8,8,128]{3,2,1,0:T(8,128)(2,1)S(1)}, u32[]{:S(2)}, u32[]{:S(2)}) collective-permute-start(bf16[4,8,8,128]{3,2,1,0:T(8,128)(2,1)} %get-tuple-element.513), channel_id=1, source_target_pairs={{64,0},{128,64},{192,128},{256,192},{320,256},{384,320},{448,384},... | collective-permute-start | bytes 196616 | tf_op jit(solution)/shard_map/while/body/eval_jaxpr/ppermute | solution.py:14
  96.9 5.2 %collective-permute-start = (bf16[4,8,8,128]{3,2,1,0:T(8,128)(2,1)}, bf16[4,8,8,128]{3,2,1,0:T(8,128)(2,1)S(1)}, u32[]{:S(2)}, u32[]{:S(2)}) collective-permute-start(bf16[4,8,8,128]{3,2,1,0:T(8,128)(2,1)} %get-tuple-element.513), channel_id=1, source_target_pairs={{64,0},{128,64},{192,128},{256,192},{320,256},{384,320},{448,384},... | collective-permute-start | bytes 196616 | tf_op jit(solution)/shard_map/while/body/eval_jaxpr/ppermute | solution.py:14
  102.8 5.2 %collective-permute-start = (bf16[4,8,8,128]{3,2,1,0:T(8,128)(2,1)}, bf16[4,8,8,128]{3,2,1,0:T(8,128)(2,1)S(1)}, u32[]{:S(2)}, u32[]{:S(2)}) collective-permute-start(bf16[4,8,8,128]{3,2,1,0:T(8,128)(2,1)} %get-tuple-element.513), channel_id=1, source_target_pairs={{64,0},{128,64},{192,128},{256,192},{320,256},{384,320},{448,384},... | collective-permute-start | bytes 196616 | tf_op jit(solution)/shard_map/while/body/eval_jaxpr/ppermute | solution.py:14
  108.6 7.8 %collective-permute-start = (bf16[4,8,8,128]{3,2,1,0:T(8,128)(2,1)}, bf16[4,8,8,128]{3,2,1,0:T(8,128)(2,1)S(1)}, u32[]{:S(2)}, u32[]{:S(2)}) collective-permute-start(bf16[4,8,8,128]{3,2,1,0:T(8,128)(2,1)} %get-tuple-element.513), channel_id=1, source_target_pairs={{64,0},{128,64},{192,128},{256,192},{320,256},{384,320},{448,384},... | collective-permute-start | bytes 196616 | tf_op jit(solution)/shard_map/while/body/eval_jaxpr/ppermute | solution.py:14
  117.1 8.8 %collective-permute-start = (bf16[4,8,8,128]{3,2,1,0:T(8,128)(2,1)}, bf16[4,8,8,128]{3,2,1,0:T(8,128)(2,1)S(1)}, u32[]{:S(2)}, u32[]{:S(2)}) collective-permute-start(bf16[4,8,8,128]{3,2,1,0:T(8,128)(2,1)} %get-tuple-element.513), channel_id=1, source_target_pairs={{64,0},{128,64},{192,128},{256,192},{320,256},{384,320},{448,384},... | collective-permute-start | bytes 196616 | tf_op jit(solution)/shard_map/while/body/eval_jaxpr/ppermute | solution.py:14
  126.5 8.8 %collective-permute-start = (bf16[4,8,8,128]{3,2,1,0:T(8,128)(2,1)}, bf16[4,8,8,128]{3,2,1,0:T(8,128)(2,1)S(1)}, u32[]{:S(2)}, u32[]{:S(2)}) collective-permute-start(bf16[4,8,8,128]{3,2,1,0:T(8,128)(2,1)} %get-tuple-element.513), channel_id=1, source_target_pairs={{64,0},{128,64},{192,128},{256,192},{320,256},{384,320},{448,384},... | collective-permute-start | bytes 196616 | tf_op jit(solution)/shard_map/while/body/eval_jaxpr/ppermute | solution.py:14
  136.0 73.2 %collective-permute-start = (bf16[4,8,8,128]{3,2,1,0:T(8,128)(2,1)}, bf16[4,8,8,128]{3,2,1,0:T(8,128)(2,1)S(1)}, u32[]{:S(2)}, u32[]{:S(2)}) collective-permute-start(bf16[4,8,8,128]{3,2,1,0:T(8,128)(2,1)} %get-tuple-element.513), channel_id=1, source_target_pairs={{64,0},{128,64},{192,128},{256,192},{320,256},{384,320},{448,384},... | collective-permute-start | bytes 196616 | tf_op jit(solution)/shard_map/while/body/eval_jaxpr/ppermute | solution.py:14
  221.1 8.8 %collective-permute-start = (bf16[4,8,8,128]{3,2,1,0:T(8,128)(2,1)}, bf16[4,8,8,128]{3,2,1,0:T(8,128)(2,1)S(1)}, u32[]{:S(2)}, u32[]{:S(2)}) collective-permute-start(bf16[4,8,8,128]{3,2,1,0:T(8,128)(2,1)} %get-tuple-element.513), channel_id=1, source_target_pairs={{64,0},{128,64},{192,128},{256,192},{320,256},{384,320},{448,384},... | collective-permute-start | bytes 196616 | tf_op jit(solution)/shard_map/while/body/eval_jaxpr/ppermute | solution.py:14
  241.9 5.2 %collective-permute-start = (bf16[4,8,8,128]{3,2,1,0:T(8,128)(2,1)}, bf16[4,8,8,128]{3,2,1,0:T(8,128)(2,1)S(1)}, u32[]{:S(2)}, u32[]{:S(2)}) collective-permute-start(bf16[4,8,8,128]{3,2,1,0:T(8,128)(2,1)} %get-tuple-element.513), channel_id=1, source_target_pairs={{64,0},{128,64},{192,128},{256,192},{320,256},{384,320},{448,384},... | collective-permute-start | bytes 196616 | tf_op jit(solution)/shard_map/while/body/eval_jaxpr/ppermute | solution.py:14
  381.1 24.9 %collective-permute-start.9 = (f32[64,128]{1,0:T(8,128)S(1)}, f32[64,128]{1,0:T(8,128)S(1)}, u32[]{:S(2)}, u32[]{:S(2)}) collective-permute-start(f32[64,128]{1,0:T(8,128)S(1)} %fusion), channel_id=1, source_target_pairs={{0,9},{1,10},{2,11},{3,12},{4,13},{5,14},{6,15},{7,16},{8,17},{9,1... | collective-permute-start | bytes 98312
  382.4 33.2 %collective-permute-start.8 = (f32[64,128]{1,0:T(8,128)S(1)}, f32[64,128]{1,0:T(8,128)S(1)}, u32[]{:S(2)}, u32[]{:S(2)}) collective-permute-start(f32[64,128]{1,0:T(8,128)S(1)} %fusion), channel_id=1, source_target_pairs={{0,8},{1,9},{2,10},{3,11},{4,12},{5,13},{6,14},{7,15},{8,16},{9,17... | collective-permute-start | bytes 98312
  383.7 33.3 %collective-permute-start.7 = (f32[64,128]{1,0:T(8,128)S(1)}, f32[64,128]{1,0:T(8,128)S(1)}, u32[]{:S(2)}, u32[]{:S(2)}) collective-permute-start(f32[64,128]{1,0:T(8,128)S(1)} %fusion), channel_id=1, source_target_pairs={{0,7},{1,8},{2,9},{3,10},{4,11},{5,12},{6,13},{7,14},{8,15},{9,16}... | collective-permute-start | bytes 98312
  385.0 35.1 %collective-permute-start.6 = (f32[64,128]{1,0:T(8,128)S(1)}, f32[64,128]{1,0:T(8,128)S(1)}, u32[]{:S(2)}, u32[]{:S(2)}) collective-permute-start(f32[64,128]{1,0:T(8,128)S(1)} %fusion), channel_id=1, source_target_pairs={{0,6},{1,7},{2,8},{3,9},{4,10},{5,11},{6,12},{7,13},{8,14},{9,15},... | collective-permute-start | bytes 98312
  396.3 7.7 %collective-permute-start.10 = (f32[54,128]{1,0:T(8,128)S(1)}, f32[54,128]{1,0:T(8,128)S(1)}, u32[]{:S(2)}, u32[]{:S(2)}) collective-permute-start(f32[54,128]{1,0:T(8,128)S(1)} %slice.604), channel_id=1, source_target_pairs={{0,10},{1,11},{2,12},{3,13},{4,14},{5,15},{6,16},{7,17},{8,18},{9,... | collective-permute-start | bytes 82952
  404.0 22.1 %collective-permute-start.5 = (f32[64,128]{1,0:T(8,128)S(1)}, f32[64,128]{1,0:T(8,128)S(1)}, u32[]{:S(2)}, u32[]{:S(2)}) collective-permute-start(f32[64,128]{1,0:T(8,128)S(1)} %fusion), channel_id=1, source_target_pairs={{0,5},{1,6},{2,7},{3,8},{4,9},{5,10},{6,11},{7,12},{8,13},{9,14},{... | collective-permute-start | bytes 98312
  406.0 20.1 %collective-permute-start.4 = (f32[64,128]{1,0:T(8,128)S(1)}, f32[64,128]{1,0:T(8,128)S(1)}, u32[]{:S(2)}, u32[]{:S(2)}) collective-permute-start(f32[64,128]{1,0:T(8,128)S(1)} %fusion), channel_id=1, source_target_pairs={{0,4},{1,5},{2,6},{3,7},{4,8},{5,9},{6,10},{7,11},{8,12},{9,13},{1... | collective-permute-start | bytes 98312
  415.6 10.4 %collective-permute-start.3 = (f32[64,128]{1,0:T(8,128)S(1)}, f32[64,128]{1,0:T(8,128)S(1)}, u32[]{:S(2)}, u32[]{:S(2)}) collective-permute-start(f32[64,128]{1,0:T(8,128)S(1)} %fusion), channel_id=1, source_target_pairs={{0,3},{1,4},{2,5},{3,6},{4,7},{5,8},{6,9},{7,10},{8,11},{9,12},{10... | collective-permute-start | bytes 98312
  416.9 9.1 %collective-permute-start.2 = (f32[64,128]{1,0:T(8,128)S(1)}, f32[64,128]{1,0:T(8,128)S(1)}, u32[]{:S(2)}, u32[]{:S(2)}) collective-permute-start(f32[64,128]{1,0:T(8,128)S(1)} %fusion), channel_id=1, source_target_pairs={{0,2},{1,3},{2,4},{3,5},{4,6},{5,7},{6,8},{7,9},{8,10},{9,11},{10,... | collective-permute-start | bytes 98312
  420.1 6.0 %collective-permute-start.1 = (f32[64,128]{1,0:T(8,128)S(1)}, f32[64,128]{1,0:T(8,128)S(1)}, u32[]{:S(2)}, u32[]{:S(2)}) collective-permute-start(f32[64,128]{1,0:T(8,128)S(1)} %fusion), channel_id=1, source_target_pairs={{0,1},{1,2},{2,3},{3,4},{4,5},{5,6},{6,7},{7,8},{8,9},{9,10},{10,1... | collective-permute-start | bytes 98312
  (47 other events, 780.0 us)
where the time goes:
time: 429 us; the launch traced here: 428 us
  blocking collectives  198 us (46%)
  waiting for transfers between devices  119 us (28%)
  starting transfers between devices  52.7 us (12%)
  matrix products  29.6 us (7%)
  local copies, waits for them, and re-layouts  20.6 us (5%)
  other arithmetic  5.32 us (1%)
    unnamed x1, blocking collectives  122 us
    ppermute x9, waiting for transfers between devices, passed_along(): return lax.ppermute(array, axis, pairs)  117 us
    all_gather x1, blocking collectives, local(): gathered = lax.all_gather(weights[0], 'dp', axis=0, tiled=True)  75.9 us
    unnamed x10, starting transfers between devices  41.2 us
    dot_general x108, matrix products, apply_taps(): jnp.dot(window_rows, kernel_taps[tap_index], preferred_element_type=jnp.f...  19.1 us
    ppermute x9, starting transfers between devices, passed_along(): return lax.ppermute(array, axis, pairs)  11.5 us
    dot_general x54, matrix products, tap_grads(): jnp.dot(window_rows.T, slope, preferred_element_type=jnp.float32)  10.4 us
  transfers between devices with their start and end apart: 19, of which 10 were waited for; matrix products, arithmetic and copies ran while one was open for 0% of the time, Pallas kernels for 0%

commit v1 on v0

--- a/solution.py
+++ b/solution.py
@@ -70,7 +70,9 @@
     segments = lax.axis_size("segment")
     dp_count = lax.axis_size("dp")
     segment_index = lax.axis_index("segment")
-    gathered = lax.all_gather(weights[0], "dp", axis=0, tiled=True)
+    x = weights[0]
+    outgoing = jnp.stack([x] * lax.axis_size("dp"))
+    gathered = jnp.concatenate(lax.all_to_all(outgoing, "dp", 0, 0), axis=0)
     channels = gathered.shape[1]
     kernel_taps = gathered.reshape(-1, channels, channels)
     flipped = jnp.transpose(jnp.flip(kernel_taps, 0), (0, 2, 1))

time: 429 us -> 412 us (0.960)
  blocking collectives: 198 us -> 124 us
  waiting for transfers between devices: 119 us -> 153 us
  starting transfers between devices: 52.7 us -> 74.5 us
    all_gather x1 -> x0, blocking collectives: 75.9 us -> none  [local(): gathered = lax.all_gather(weights[0], 'dp', axis=0, tiled=True)]
    all_to_all x0 -> x1, waiting for transfers between devices: none -> 35.7 us  [local(): gathered = jnp.concatenate(lax.all_to_all(outgoing, 'dp', 0, 0), axis=0)]
    all_to_all x0 -> x1, starting transfers between devices: none -> 18.2 us  [local(): gathered = jnp.concatenate(lax.all_to_all(outgoing, 'dp', 0, 0), axis=0)]
  transfers between devices with their start and end apart: 19 -> 20, of which waited for: 10 -> 11; matrix products, arithmetic and copies ran while one was open for 0% -> 3% of each run, Pallas kernels for 0% -> 0%
where the time goes in v1:
time: 412 us; the launch traced here: 411 us
  waiting for transfers between devices  153 us (37%)
  blocking collectives  124 us (30%)
  starting transfers between devices  74.5 us (18%)
  matrix products  29.5 us (7%)
  local copies, waits for them, and re-layouts  20.9 us (5%)
  other arithmetic  5.31 us (1%)
    unnamed x1, blocking collectives  124 us
    ppermute x9, waiting for transfers between devices, passed_along(): return lax.ppermute(array, axis, pairs)  116 us
    unnamed x10, starting transfers between devices  44.8 us
    all_to_all x1, waiting for transfers between devices, local(): gathered = jnp.concatenate(lax.all_to_all(outgoing, 'dp', 0, 0), axis=0)  35.7 us
    dot_general x108, matrix products, apply_taps(): jnp.dot(window_rows, kernel_taps[tap_index], preferred_element_type=jnp.f...  19.1 us
    all_to_all x1, starting transfers between devices, local(): gathered = jnp.concatenate(lax.all_to_all(outgoing, 'dp', 0, 0), axis=0)  18.2 us
    ppermute x9, starting transfers between devices, passed_along(): return lax.ppermute(array, axis, pairs)  11.5 us
    dot_general x54, matrix products, tap_grads(): jnp.dot(window_rows.T, slope, preferred_element_type=jnp.float32)  10.4 us
  transfers between devices with their start and end apart: 20, of which 11 were waited for; matrix products, arithmetic and copies ran while one was open for 3% of the time, Pallas kernels for 0%

profile of v1, /device:TPU:1, one launch (start us, length us, event | category | flops | bytes accessed | tf_op | source)
XLA Modules:
  0.0 410.8 jit_solution(506353003627990430)
XLA Ops:
  0.7 1.8 stack.6
  2.5 18.2 %all-to-all-start = ((bf16[64,54,128]{2,1,0:T(8,128)(2,1)}), bf16[64,54,128]{2,1,0:T(8,128)(2,1)S(1)}, u32[]{:S(2)}, u32[]{:S(2)}) async-start(bf16[64,54,128]{2,1,0:T(8,128)(2,1)} %stack.6), calls=%async_computation | async-start | bytes 1835008 | tf_op jit(solution)/shard_map/all_to_all | solution.py:75
  30.3 35.7 %all-to-all-done = bf16[64,54,128]{2,1,0:T(8,128)(2,1)S(1)} async-done(((bf16[64,54,128]{2,1,0:T(8,128)(2,1)}), bf16[64,54,128]{2,1,0:T(8,128)(2,1)S(1)}, u32[]{:S(2)}, u32[]{:S(2)}) %all-to-all-start) | async-done | bytes 884768 | tf_op jit(solution)/shard_map/all_to_all | solution.py:75
  68.5 156.3 %while.18 = (s32[]{:T(128)}, bf16[4,8,8,128]{3,2,1,0:T(8,128)(2,1)S(1)}, bf16[2,4,8,8,128]{4,3,2,1,0:T(8,128)(2,1)}, bf16[2,256,128]{2,1,0:T(8,128)(2,1)S(1)}, s...) while((s32[]{:T(128)}, ...), condition=%wide.region_3.4_spmd, body=%wide.region_0.3_spmd.sunk | while | flops 455180288 | bytes 23921024 | solution.py:136
  70.4 3.9 collective-permute-done
  76.3 3.9 collective-permute-done
  82.1 3.9 collective-permute-done
  87.9 6.5 %collective-permute-done = bf16[4,8,8,128]{3,2,1,0:T(8,128)(2,1)S(1)} collective-permute-done((bf16[4,8,8,128]{3,2,1,0:T(8,128)(2,1)}, bf16[4,8,8,128]{3,2,1,0:T(8,128)(2,1)S(1)}, u32[]{:S(2)}, u32[]{:S(2)}) %collective-permute-start) | collective-permute-done | bytes 65568 | tf_op jit(solution)/shard_map/while/body/eval_jaxpr/ppermute | solution.py:14
  96.4 7.5 %collective-permute-done = bf16[4,8,8,128]{3,2,1,0:T(8,128)(2,1)S(1)} collective-permute-done((bf16[4,8,8,128]{3,2,1,0:T(8,128)(2,1)}, bf16[4,8,8,128]{3,2,1,0:T(8,128)(2,1)S(1)}, u32[]{:S(2)}, u32[]{:S(2)}) %collective-permute-start) | collective-permute-done | bytes 65568 | tf_op jit(solution)/shard_map/while/body/eval_jaxpr/ppermute | solution.py:14
  105.8 7.5 %collective-permute-done = bf16[4,8,8,128]{3,2,1,0:T(8,128)(2,1)S(1)} collective-permute-done((bf16[4,8,8,128]{3,2,1,0:T(8,128)(2,1)}, bf16[4,8,8,128]{3,2,1,0:T(8,128)(2,1)S(1)}, u32[]{:S(2)}, u32[]{:S(2)}) %collective-permute-start) | collective-permute-done | bytes 65568 | tf_op jit(solution)/shard_map/while/body/eval_jaxpr/ppermute | solution.py:14
  115.3 71.6 %collective-permute-done = bf16[4,8,8,128]{3,2,1,0:T(8,128)(2,1)S(1)} collective-permute-done((bf16[4,8,8,128]{3,2,1,0:T(8,128)(2,1)}, bf16[4,8,8,128]{3,2,1,0:T(8,128)(2,1)S(1)}, u32[]{:S(2)}, u32[]{:S(2)}) %collective-permute-start) | collective-permute-done | bytes 65568 | tf_op jit(solution)/shard_map/while/body/eval_jaxpr/ppermute | solution.py:14
  186.9 11.9 %conditional.2 = (bf16[4,8,8,128]{3,2,1,0:T(8,128)(2,1)}, bf16[2,4,8,8,128]{4,3,2,1,0:T(8,128)(2,1)}, bf16[2,256,128]{2,1,0:T(8,128)(2,1)S(1)}) conditional(s32[]{:T(128)} %convert_element_type.107, (bf16[2,4,8,8,128]{4,3,2,1,0:T(8,128)(2,1)}, bf16[2,256,128]{2,1,0:T(8,128)(2,1)S(1)}) %tuple.171, (s32[]{:T(128)}, s32[]{:T(128)}, ...), branch_computations={%region_1.1_spmd, %region_2.2_spmd} | conditional | flops 455180288 | bytes 23658574 | solution.py:124
  197.3 1.5 constant_dynamic-update-slice_fusion
  200.1 7.5 %collective-permute-done = bf16[4,8,8,128]{3,2,1,0:T(8,128)(2,1)S(1)} collective-permute-done((bf16[4,8,8,128]{3,2,1,0:T(8,128)(2,1)}, bf16[4,8,8,128]{3,2,1,0:T(8,128)(2,1)S(1)}, u32[]{:S(2)}, u32[]{:S(2)}) %collective-permute-start) | collective-permute-done | bytes 65568 | tf_op jit(solution)/shard_map/while/body/eval_jaxpr/ppermute | solution.py:14
  207.6 11.9 %conditional.2 = (bf16[4,8,8,128]{3,2,1,0:T(8,128)(2,1)}, bf16[2,4,8,8,128]{4,3,2,1,0:T(8,128)(2,1)}, bf16[2,256,128]{2,1,0:T(8,128)(2,1)S(1)}) conditional(s32[]{:T(128)} %convert_element_type.107, (bf16[2,4,8,8,128]{4,3,2,1,0:T(8,128)(2,1)}, bf16[2,256,128]{2,1,0:T(8,128)(2,1)S(1)}) %tuple.171, (s32[]{:T(128)}, s32[]{:T(128)}, ...), branch_computations={%region_1.1_spmd, %region_2.2_spmd} | conditional | flops 455180288 | bytes 23658574 | solution.py:124
  220.8 3.9 collective-permute-done
  236.4 124.2 %fusion = f32[64,128]{1,0:T(8,128)S(1)} fusion(f32[3456,128]{1,0:T(8,128)S(1)} %add.436), kind=kCustom, calls=%all-reduce-scatter | all-reduce-scatter fusion | flops 524289 | bytes 1804288
  364.6 14.2 %collective-permute-start.6 = (f32[64,128]{1,0:T(8,128)S(1)}, f32[64,128]{1,0:T(8,128)S(1)}, u32[]{:S(2)}, u32[]{:S(2)}) collective-permute-start(f32[64,128]{1,0:T(8,128)S(1)} %fusion), channel_id=1, source_target_pairs={{0,6},{1,7},{2,8},{3,9},{4,10},{5,11},{6,12},{7,13},{8,14},{9,15},... | collective-permute-start | bytes 98312
  378.8 6.0 %collective-permute-start.10 = (f32[54,128]{1,0:T(8,128)S(1)}, f32[54,128]{1,0:T(8,128)S(1)}, u32[]{:S(2)}, u32[]{:S(2)}) collective-permute-start(f32[54,128]{1,0:T(8,128)S(1)} %slice.604), channel_id=1, source_target_pairs={{0,10},{1,11},{2,12},{3,13},{4,14},{5,15},{6,16},{7,17},{8,18},{9,... | collective-permute-start | bytes 82952
  385.8 3.2 collective-permute-start.5
  389.0 8.8 %collective-permute-start.4 = (f32[64,128]{1,0:T(8,128)S(1)}, f32[64,128]{1,0:T(8,128)S(1)}, u32[]{:S(2)}, u32[]{:S(2)}) collective-permute-start(f32[64,128]{1,0:T(8,128)S(1)} %fusion), channel_id=1, source_target_pairs={{0,4},{1,5},{2,6},{3,7},{4,8},{5,9},{6,10},{7,11},{8,12},{9,13},{1... | collective-permute-start | bytes 98312
  399.1 3.1 collective-permute-start.2
  402.3 4.2 %collective-permute-start.1 = (f32[64,128]{1,0:T(8,128)S(1)}, f32[64,128]{1,0:T(8,128)S(1)}, u32[]{:S(2)}, u32[]{:S(2)}) collective-permute-start(f32[64,128]{1,0:T(8,128)S(1)} %fusion), channel_id=1, source_target_pairs={{0,1},{1,2},{2,3},{3,4},{4,5},{5,6},{6,7},{7,8},{8,9},{9,10},{10,1... | collective-permute-start | bytes 98312
  408.4 1.7 concatenate.8
  (345 shorter events, 72.9 us)
Async XLA Ops:
  2.5 63.5 %all-to-all-start = ((bf16[64,54,128]{2,1,0:T(8,128)(2,1)}), bf16[64,54,128]{2,1,0:T(8,128)(2,1)S(1)}, u32[]{:S(2)}, u32[]{:S(2)}) async-start(bf16[64,54,128]{2,1,0:T(8,128)(2,1)} %stack.6), calls=%async_computation | async-start | bytes 1835008 | tf_op jit(solution)/shard_map/all_to_all | solution.py:75
  68.5 157.4 %copy-start.43 = (bf16[4,8,8,128]{3,2,1,0:T(8,128)(2,1)S(1)}, bf16[4,8,8,128]{3,2,1,0:T(8,128)(2,1)}, u32[]{:S(2)}) copy-start(bf16[4,8,8,128]{3,2,1,0:T(8,128)(2,1)} %get-tuple-element.406) | copy-start | bytes 196612
  68.5 157.6 %copy-start.42 = (bf16[4,8,8,128]{3,2,1,0:T(8,128)(2,1)S(1)}, bf16[4,8,8,128]{3,2,1,0:T(8,128)(2,1)}, u32[]{:S(2)}) copy-start(bf16[4,8,8,128]{3,2,1,0:T(8,128)(2,1)} %get-tuple-element.407) | copy-start | bytes 196612
  68.5 157.8 %copy-start.41 = (bf16[4,8,8,128]{3,2,1,0:T(8,128)(2,1)S(1)}, bf16[4,8,8,128]{3,2,1,0:T(8,128)(2,1)}, u32[]{:S(2)}) copy-start(bf16[4,8,8,128]{3,2,1,0:T(8,128)(2,1)} %get-tuple-element.408) | copy-start | bytes 196612
  68.5 158.1 %copy-start.39 = (bf16[4,8,8,128]{3,2,1,0:T(8,128)(2,1)S(1)}, bf16[4,8,8,128]{3,2,1,0:T(8,128)(2,1)}, u32[]{:S(2)}) copy-start(bf16[4,8,8,128]{3,2,1,0:T(8,128)(2,1)} %get-tuple-element.409) | copy-start | bytes 196612
  69.2 5.2 %collective-permute-start = (bf16[4,8,8,128]{3,2,1,0:T(8,128)(2,1)}, bf16[4,8,8,128]{3,2,1,0:T(8,128)(2,1)S(1)}, u32[]{:S(2)}, u32[]{:S(2)}) collective-permute-start(bf16[4,8,8,128]{3,2,1,0:T(8,128)(2,1)} %get-tuple-element.524), channel_id=1, source_target_pairs={{64,0},{128,64},{192,128},{256,192},{320,256},{384,320},{448,384},... | collective-permute-start | bytes 196616 | tf_op jit(solution)/shard_map/while/body/eval_jaxpr/ppermute | solution.py:14
  75.0 5.2 %collective-permute-start = (bf16[4,8,8,128]{3,2,1,0:T(8,128)(2,1)}, bf16[4,8,8,128]{3,2,1,0:T(8,128)(2,1)S(1)}, u32[]{:S(2)}, u32[]{:S(2)}) collective-permute-start(bf16[4,8,8,128]{3,2,1,0:T(8,128)(2,1)} %get-tuple-element.524), channel_id=1, source_target_pairs={{64,0},{128,64},{192,128},{256,192},{320,256},{384,320},{448,384},... | collective-permute-start | bytes 196616 | tf_op jit(solution)/shard_map/while/body/eval_jaxpr/ppermute | solution.py:14
  80.8 5.2 %collective-permute-start = (bf16[4,8,8,128]{3,2,1,0:T(8,128)(2,1)}, bf16[4,8,8,128]{3,2,1,0:T(8,128)(2,1)S(1)}, u32[]{:S(2)}, u32[]{:S(2)}) collective-permute-start(bf16[4,8,8,128]{3,2,1,0:T(8,128)(2,1)} %get-tuple-element.524), channel_id=1, source_target_pairs={{64,0},{128,64},{192,128},{256,192},{320,256},{384,320},{448,384},... | collective-permute-start | bytes 196616 | tf_op jit(solution)/shard_map/while/body/eval_jaxpr/ppermute | solution.py:14
  86.6 7.8 %collective-permute-start = (bf16[4,8,8,128]{3,2,1,0:T(8,128)(2,1)}, bf16[4,8,8,128]{3,2,1,0:T(8,128)(2,1)S(1)}, u32[]{:S(2)}, u32[]{:S(2)}) collective-permute-start(bf16[4,8,8,128]{3,2,1,0:T(8,128)(2,1)} %get-tuple-element.524), channel_id=1, source_target_pairs={{64,0},{128,64},{192,128},{256,192},{320,256},{384,320},{448,384},... | collective-permute-start | bytes 196616 | tf_op jit(solution)/shard_map/while/body/eval_jaxpr/ppermute | solution.py:14
  95.1 8.8 %collective-permute-start = (bf16[4,8,8,128]{3,2,1,0:T(8,128)(2,1)}, bf16[4,8,8,128]{3,2,1,0:T(8,128)(2,1)S(1)}, u32[]{:S(2)}, u32[]{:S(2)}) collective-permute-start(bf16[4,8,8,128]{3,2,1,0:T(8,128)(2,1)} %get-tuple-element.524), channel_id=1, source_target_pairs={{64,0},{128,64},{192,128},{256,192},{320,256},{384,320},{448,384},... | collective-permute-start | bytes 196616 | tf_op jit(solution)/shard_map/while/body/eval_jaxpr/ppermute | solution.py:14
  104.5 8.8 %collective-permute-start = (bf16[4,8,8,128]{3,2,1,0:T(8,128)(2,1)}, bf16[4,8,8,128]{3,2,1,0:T(8,128)(2,1)S(1)}, u32[]{:S(2)}, u32[]{:S(2)}) collective-permute-start(bf16[4,8,8,128]{3,2,1,0:T(8,128)(2,1)} %get-tuple-element.524), channel_id=1, source_target_pairs={{64,0},{128,64},{192,128},{256,192},{320,256},{384,320},{448,384},... | collective-permute-start | bytes 196616 | tf_op jit(solution)/shard_map/while/body/eval_jaxpr/ppermute | solution.py:14
  114.0 72.9 %collective-permute-start = (bf16[4,8,8,128]{3,2,1,0:T(8,128)(2,1)}, bf16[4,8,8,128]{3,2,1,0:T(8,128)(2,1)S(1)}, u32[]{:S(2)}, u32[]{:S(2)}) collective-permute-start(bf16[4,8,8,128]{3,2,1,0:T(8,128)(2,1)} %get-tuple-element.524), channel_id=1, source_target_pairs={{64,0},{128,64},{192,128},{256,192},{320,256},{384,320},{448,384},... | collective-permute-start | bytes 196616 | tf_op jit(solution)/shard_map/while/body/eval_jaxpr/ppermute | solution.py:14
  198.8 8.8 %collective-permute-start = (bf16[4,8,8,128]{3,2,1,0:T(8,128)(2,1)}, bf16[4,8,8,128]{3,2,1,0:T(8,128)(2,1)S(1)}, u32[]{:S(2)}, u32[]{:S(2)}) collective-permute-start(bf16[4,8,8,128]{3,2,1,0:T(8,128)(2,1)} %get-tuple-element.524), channel_id=1, source_target_pairs={{64,0},{128,64},{192,128},{256,192},{320,256},{384,320},{448,384},... | collective-permute-start | bytes 196616 | tf_op jit(solution)/shard_map/while/body/eval_jaxpr/ppermute | solution.py:14
  219.5 5.2 %collective-permute-start = (bf16[4,8,8,128]{3,2,1,0:T(8,128)(2,1)}, bf16[4,8,8,128]{3,2,1,0:T(8,128)(2,1)S(1)}, u32[]{:S(2)}, u32[]{:S(2)}) collective-permute-start(bf16[4,8,8,128]{3,2,1,0:T(8,128)(2,1)} %get-tuple-element.524), channel_id=1, source_target_pairs={{64,0},{128,64},{192,128},{256,192},{320,256},{384,320},{448,384},... | collective-permute-start | bytes 196616 | tf_op jit(solution)/shard_map/while/body/eval_jaxpr/ppermute | solution.py:14
  360.6 28.4 %collective-permute-start.9 = (f32[64,128]{1,0:T(8,128)S(1)}, f32[64,128]{1,0:T(8,128)S(1)}, u32[]{:S(2)}, u32[]{:S(2)}) collective-permute-start(f32[64,128]{1,0:T(8,128)S(1)} %fusion), channel_id=1, source_target_pairs={{0,9},{1,10},{2,11},{3,12},{4,13},{5,14},{6,15},{7,16},{8,17},{9,1... | collective-permute-start | bytes 98312
  361.9 36.0 %collective-permute-start.8 = (f32[64,128]{1,0:T(8,128)S(1)}, f32[64,128]{1,0:T(8,128)S(1)}, u32[]{:S(2)}, u32[]{:S(2)}) collective-permute-start(f32[64,128]{1,0:T(8,128)S(1)} %fusion), channel_id=1, source_target_pairs={{0,8},{1,9},{2,10},{3,11},{4,12},{5,13},{6,14},{7,15},{8,16},{9,17... | collective-permute-start | bytes 98312
  363.2 36.0 %collective-permute-start.7 = (f32[64,128]{1,0:T(8,128)S(1)}, f32[64,128]{1,0:T(8,128)S(1)}, u32[]{:S(2)}, u32[]{:S(2)}) collective-permute-start(f32[64,128]{1,0:T(8,128)S(1)} %fusion), channel_id=1, source_target_pairs={{0,7},{1,8},{2,9},{3,10},{4,11},{5,12},{6,13},{7,14},{8,15},{9,16}... | collective-permute-start | bytes 98312
  364.6 37.7 %collective-permute-start.6 = (f32[64,128]{1,0:T(8,128)S(1)}, f32[64,128]{1,0:T(8,128)S(1)}, u32[]{:S(2)}, u32[]{:S(2)}) collective-permute-start(f32[64,128]{1,0:T(8,128)S(1)} %fusion), channel_id=1, source_target_pairs={{0,6},{1,7},{2,8},{3,9},{4,10},{5,11},{6,12},{7,13},{8,14},{9,15},... | collective-permute-start | bytes 98312
  378.8 6.9 %collective-permute-start.10 = (f32[54,128]{1,0:T(8,128)S(1)}, f32[54,128]{1,0:T(8,128)S(1)}, u32[]{:S(2)}, u32[]{:S(2)}) collective-permute-start(f32[54,128]{1,0:T(8,128)S(1)} %slice.604), channel_id=1, source_target_pairs={{0,10},{1,11},{2,12},{3,13},{4,14},{5,15},{6,16},{7,17},{8,18},{9,... | collective-permute-start | bytes 82952
  385.8 22.6 %collective-permute-start.5 = (f32[64,128]{1,0:T(8,128)S(1)}, f32[64,128]{1,0:T(8,128)S(1)}, u32[]{:S(2)}, u32[]{:S(2)}) collective-permute-start(f32[64,128]{1,0:T(8,128)S(1)} %fusion), channel_id=1, source_target_pairs={{0,5},{1,6},{2,7},{3,8},{4,9},{5,10},{6,11},{7,12},{8,13},{9,14},{... | collective-permute-start | bytes 98312
  389.0 19.4 %collective-permute-start.4 = (f32[64,128]{1,0:T(8,128)S(1)}, f32[64,128]{1,0:T(8,128)S(1)}, u32[]{:S(2)}, u32[]{:S(2)}) collective-permute-start(f32[64,128]{1,0:T(8,128)S(1)} %fusion), channel_id=1, source_target_pairs={{0,4},{1,5},{2,6},{3,7},{4,8},{5,9},{6,10},{7,11},{8,12},{9,13},{1... | collective-permute-start | bytes 98312
  397.8 10.6 %collective-permute-start.3 = (f32[64,128]{1,0:T(8,128)S(1)}, f32[64,128]{1,0:T(8,128)S(1)}, u32[]{:S(2)}, u32[]{:S(2)}) collective-permute-start(f32[64,128]{1,0:T(8,128)S(1)} %fusion), channel_id=1, source_target_pairs={{0,3},{1,4},{2,5},{3,6},{4,7},{5,8},{6,9},{7,10},{8,11},{9,12},{10... | collective-permute-start | bytes 98312
  399.1 9.3 %collective-permute-start.2 = (f32[64,128]{1,0:T(8,128)S(1)}, f32[64,128]{1,0:T(8,128)S(1)}, u32[]{:S(2)}, u32[]{:S(2)}) collective-permute-start(f32[64,128]{1,0:T(8,128)S(1)} %fusion), channel_id=1, source_target_pairs={{0,2},{1,3},{2,4},{3,5},{4,6},{5,7},{6,8},{7,9},{8,10},{9,11},{10,... | collective-permute-start | bytes 98312
  402.3 6.1 %collective-permute-start.1 = (f32[64,128]{1,0:T(8,128)S(1)}, f32[64,128]{1,0:T(8,128)S(1)}, u32[]{:S(2)}, u32[]{:S(2)}) collective-permute-start(f32[64,128]{1,0:T(8,128)S(1)} %fusion), channel_id=1, source_target_pairs={{0,1},{1,2},{2,3},{3,4},{4,5},{5,6},{6,7},{7,8},{8,9},{9,10},{10,1... | collective-permute-start | bytes 98312
  (47 other events, 993.6 us)
